TPU v7x, 128 devices: a whole 4x4x4 slice. The times are simulated.
128 devices in a mesh: tok: 16 (over y, x), head: 8 (over z, core).
Axes of the slice: x: 4, y: 4, z: 4, core: 2. Of those that a mesh axis runs over, the one named last changes fastest.
Arguments:
- tokens: bfloat16 [8192, 8192], P('tok', 'head'), may hold values from -60 to 60
- gain: bfloat16 [8192], P('head'), may hold values from 0.5 to 2
- w_query: bfloat16 [8192, 8, 512], P(('head', 'tok')), may hold values from -0.125 to 0.125
- w_key: bfloat16 [8192, 8, 128], P(('head', 'tok')), may hold values from -0.0625 to 0.0625
- w_value: bfloat16 [8192, 8, 128], P(('head', 'tok')), may hold values from -0.5 to 0.5
- group_ids: int32 [8192, 1], P('tok'), may hold values from 0 to 15; in each aligned block of 512 rows (0 to 511, 512 to 1023, ...) at most 64 rows name the same one
- key_pages: bfloat16 [1024, 128, 8, 128], P('tok', None, 'head'), may hold values from -42 to 42
- value_pages: bfloat16 [1024, 128, 8, 128], P('tok', None, 'head'), may hold values from -48 to 48
- page_table: int32 [16, 32], P('tok'), may hold values from 0 to 1023, as said below
Outputs:
- attention: bfloat16 [8192, 4096], P('tok', 'head')
Inputs may be any that keep to these rules, and one draw needn't show every extreme that they name: `group_ids`: among the 512 tokens of one index of tok (aligned blocks of rows), no group appears more than 64 times, a bound that some block reaches. `page_table`: row g lists 32 different pages, all in g * 64 to (g + 1) * 64 - 1, among them the first and the last page of that range.
All inputs are finite; a program needn't handle non-finite values.
Results may differ from a plain program's by a relative error of at most 0.0085.
The roundings to bfloat16 on the way count: a program that leaves them out, or rounds other values in their place, can miss the bound.
Values may be sent and summed in bfloat16 or wider, within the bound.
No kernel may reach another device: no remote copies, remote signals or barrier semaphores. Data moves between devices by JAX's collectives and lax.ppermute only.
A program may use at most 128 MiB of HBM per device.

v0:
```python
import math
import jax
import jax.numpy as jnp
from jax import lax
from jax.sharding import PartitionSpec as P

EPS = 1e-05
THETA = 10000.0


def rotate(values, positions):
    halfway = values.shape[-1] // 2
    frequency = jnp.exp(
        -math.log(THETA) * 2.0 * jnp.arange(halfway, dtype=jnp.float32) / values.shape[-1]
    )
    angles = positions.astype(jnp.float32)[:, None] * frequency[None, :]
    cosine = jnp.cos(angles)[:, None, :]
    sine_part = jnp.sin(angles)[:, None, :]
    leading = values[..., :halfway].astype(jnp.float32)
    trailing = values[..., halfway:].astype(jnp.float32)
    return jnp.concatenate(
        [leading * cosine - trailing * sine_part, trailing * cosine + leading * sine_part], axis=-1
    ).astype(jnp.bfloat16)


def attend(
    queries, query_rank, prefix_keys, prefix_values, new_keys, new_values, key_rank, key_live
):
    scaling = 1.0 / math.sqrt(queries.shape[-1])
    before = (
        jnp.einsum("bhd,pd->bhp", queries, prefix_keys, preferred_element_type=jnp.float32)
        * scaling
    )
    inside = (
        jnp.einsum("bhd,sd->bhs", queries, new_keys, preferred_element_type=jnp.float32) * scaling
    )
    allowed = key_live[None, :] & (key_rank[None, :] <= query_rank[:, None])
    inside = jnp.where(allowed[:, None, :], inside, -jnp.inf)
    highest = jnp.maximum(jnp.max(before, axis=-1), jnp.max(inside, axis=-1))
    expo_before = jnp.exp(before - highest[..., None])
    expo_inside = jnp.exp(inside - highest[..., None])
    totals = jnp.sum(expo_before, axis=-1) + jnp.sum(expo_inside, axis=-1)
    mixed = jnp.einsum(
        "bhp,pd->bhd",
        expo_before.astype(jnp.bfloat16),
        prefix_values,
        preferred_element_type=jnp.float32,
    )
    mixed = mixed + jnp.einsum(
        "bhs,sd->bhd",
        expo_inside.astype(jnp.bfloat16),
        new_values,
        preferred_element_type=jnp.float32,
    )
    return (mixed / totals[..., None]).astype(jnp.bfloat16)


def row_norm(tokens, gain, full_width):
    values_wide = tokens.astype(jnp.float32)
    squares = lax.psum(jnp.sum(values_wide * values_wide, axis=1), "head")
    factor = lax.rsqrt(squares / full_width + EPS)
    return (values_wide * factor[:, None] * gain.astype(jnp.float32)[None, :]).astype(jnp.bfloat16)


def body(tokens, gain, w_query, w_key, w_value, group_ids, key_pages, value_pages, page_table):
    row_count = tokens.shape[0]
    n_tok = lax.axis_size("tok")
    n_head = lax.axis_size("head")
    head_size = key_pages.shape[-1]
    query_width = w_query.shape[2]
    group_heads = query_width // head_size
    full_width = tokens.shape[1] * n_head
    capacity = 2 * row_count // n_tok
    normed = row_norm(tokens, gain, full_width)
    weights_local = jnp.concatenate([w_query, w_key, w_value], axis=2)
    gathered = lax.all_gather(weights_local, "tok", axis=0, tiled=True)
    group_count = row_count * lax.axis_size("head") // row_count
    joined = jnp.einsum("rd,dnc->nrc", normed, gathered, preferred_element_type=jnp.float32)
    projected = lax.psum_scatter(
        joined.reshape(group_count * row_count, joined.shape[2]),
        "head",
        scatter_dimension=0,
        tiled=True,
    )
    projected_low = projected.astype(jnp.bfloat16)
    width_all = projected_low.shape[1]
    group_of = group_ids[:, 0]
    member = (group_of[:, None] == jnp.arange(n_tok, dtype=jnp.int32)[None, :]).astype(jnp.int32)
    local_rank = jnp.sum((jnp.cumsum(member, axis=0) - member) * member, axis=1)
    slot_index = group_of * capacity + local_rank
    outgoing = (
        jnp.zeros((n_tok * capacity, width_all), jnp.bfloat16).at[slot_index].set(projected_low)
    )
    arrived = lax.all_to_all(
        outgoing.reshape(n_tok, capacity, width_all), "tok", split_axis=0, concat_axis=0, tiled=True
    )
    all_groups = lax.all_gather(group_of, "tok", axis=0, tiled=True).reshape(n_tok, row_count)
    block_counts = jnp.sum((all_groups == lax.axis_index("tok")).astype(jnp.int32), axis=1)
    slot_total = n_tok * capacity
    arrived = arrived.reshape(slot_total, width_all)
    live_count = (
        (jnp.arange(capacity, dtype=jnp.int32)[None, :] < block_counts[:, None])
        .astype(jnp.int32)
        .reshape(slot_total)
    )
    key_live = live_count > 0
    slot_rank = jnp.cumsum(live_count) - live_count
    prefix_length = page_table.shape[1] * key_pages.shape[1]
    positions = prefix_length + slot_rank
    rotated_queries = rotate(
        arrived[:, :query_width].reshape(slot_total, group_heads, head_size), positions
    )
    rotated_keys = rotate(
        arrived[:, query_width : query_width + head_size].reshape(slot_total, 1, head_size),
        positions,
    )[:, 0, :]
    slot_values = arrived[:, query_width + head_size :]
    local_pages = page_table[0] - lax.axis_index("tok") * key_pages.shape[0]
    prefix_keys = jnp.take(key_pages[:, :, 0, :], local_pages, axis=0).reshape(
        prefix_length, head_size
    )
    prefix_values = jnp.take(value_pages[:, :, 0, :], local_pages, axis=0).reshape(
        prefix_length, head_size
    )
    block_size = min(128, slot_total)

    def one_block(blocked):
        return attend(
            blocked[0],
            blocked[1],
            prefix_keys,
            prefix_values,
            rotated_keys,
            slot_values,
            slot_rank,
            key_live,
        )

    attended = lax.map(
        one_block,
        (
            rotated_queries.reshape(slot_total // block_size, block_size, group_heads, head_size),
            slot_rank.reshape(slot_total // block_size, block_size),
        ),
    )
    returned = lax.all_to_all(
        attended.reshape(n_tok, capacity, query_width),
        "tok",
        split_axis=0,
        concat_axis=0,
        tiled=True,
    )
    return returned.reshape(n_tok * capacity, query_width)[slot_index]


def solution(mesh):
    placed = (
        P("tok", "head"),
        P("head"),
        P(("head", "tok"), None, None),
        P(("head", "tok"), None, None),
        P(("head", "tok"), None, None),
        P("tok", None),
        P("tok", None, "head", None),
        P("tok", None, "head", None),
        P("tok", None),
    )
    return jax.shard_map(
        body, mesh=mesh, in_specs=placed, out_specs=P("tok", "head"), check_vma=False
    )
```

profile of v0, /device:TPU:32, one launch (start us, length us, event | category | flops | bytes accessed | tf_op | source)
XLA Modules:
  0.0 349.9 jit_solution(17621018906772747158)
XLA Ops:
  11.1 12.5 %psum.7 = f32[512]{0:T(512)S(1)} all-reduce(f32[512]{0:T(512)S(1)} %fusion.33), channel_id=1, replica_groups=mesh['tok'=16,'head'=8] {'head'}, use_global_device_ids=true, to_apply=%region_4.5 | all-reduce | flops 512 | bytes 4096 | tf_op jit(solution)/shard_map/psum | solution.py:60
  23.6 78.9 %all-gather.3.cloned.1.call-done = bf16[1024,8,768]{2,0,1:T(8,128)(2,1)} async-done(((bf16[64,8,768]{2,0,1:T(8,128)(2,1)}), bf16[1024,8,768]{2,0,1:T(8,128)(2,1)}) %all-gather.3.cloned.1.call-update) | async-done | bytes 12582928 | tf_op jit(solution)/shard_map/all_gather | solution.py:76
  102.5 14.4 %fusion.41 = f32[8,768,512]{1,2,0:T(8,128)} fusion(bf16[1024,8,768]{2,0,1:T(8,128)(2,1)} %all-gather.3.cloned.1.call-done, bf16[512,1024]{1,0:T(8,128)(2,1)S(1)} %copy-done.2, f32[1024]{0:T(1024)S(1)} %convert_element_type.78, f32[512]{0:T(512)S(1)} %add_rsqrt_fusion), kind=kOutput, calls=%fused_computation.58 | convolution fusion | flops 6444548096 | bytes 26220544 | tf_op jit(solution)/shard_map/rd,dnc->nrc/dot_general | solution.py:78
  117.6 23.0 %all-gather = s32[8192,1]{0,1:T(1,128)S(1)} all-gather(s32[512,1]{0,1:T(1,128)S(1)} %copy-done.4), channel_id=2, replica_groups=mesh['tok'=16,'head'=8] {'tok'}, dimensions={0}, use_global_device_ids=true | all-gather | bytes 34816 | tf_op jit(solution)/shard_map/all_gather | solution.py:97
  143.2 43.5 %reduce-scatter.2.cloned.1.call-done = f32[512,768]{1,0:T(8,128)} async-done(((f32[4096,768]{1,0:T(8,128)}), f32[512,768]{1,0:T(8,128)}) %reduce-scatter.2.cloned.1.call-update) | async-done | bytes 1572880 | tf_op jit(solution)/shard_map/reduce_scatter | solution.py:79
  186.7 4.6 %scatter_custom_fusion = bf16[1024,768]{1,0:T(8,128)(2,1)} fusion(s32[512]{0:T(512)S(1)} %bitcast.121, f32[512,768]{1,0:T(8,128)} %reduce-scatter.2.cloned.1.call-done, bf16[]{:T(256)} %constant.32.clone.1), kind=kCustom, calls=%fused_computation.65 | custom fusion | flops 393216 | bytes 3145730 | tf_op jit(solution)/shard_map/scatter | solution.py:92
  191.4 7.2 %all-to-all-start = ((bf16[16,64,768]{2,1,0:T(8,128)(2,1)}), bf16[16,64,768]{2,1,0:T(8,128)(2,1)}, u32[]{:S(2)}, u32[]{:S(2)}) async-start(bf16[16,64,768]{2,1,0:T(8,128)(2,1)} %bitcast.112), calls=%async_computation.1 | async-start | bytes 3145728 | tf_op jit(solution)/shard_map/all_to_all | solution.py:94
  200.3 3.2 gather_fusion.2
  205.6 2.8 broadcast_select_fusion
  208.4 18.2 %all-to-all-done = bf16[16,64,768]{2,1,0:T(8,128)(2,1)} async-done(((bf16[16,64,768]{2,1,0:T(8,128)(2,1)}), bf16[16,64,768]{2,1,0:T(8,128)(2,1)}, u32[]{:S(2)}, u32[]{:S(2)}) %all-to-all-start) | async-done | bytes 1572896 | tf_op jit(solution)/shard_map/all_to_all | solution.py:94
  228.4 2.3 slice.52
  230.6 3.1 fusion.57
  233.7 2.3 copy.21
  239.0 2.4 copy.19
  242.6 73.7 %while.11 = (s32[]{:T(128)}, bf16[8,128,4,128]{3,2,1,0:T(4,128)(2,1)}, bf16[8,128,4,128]{3,1,2,0:T(8,128)(2,1)}, bf16[4096,128]{1,0:T(8,128)(2,1)}, s32[1024]{0:...) while((s32[]{:T(128)}, ...), condition=%wide.region_15.17_spmd.clone, body=%wide.region_10.16_spmd.clone.sunk | while | flops 1365182464 | bytes 41082088 | solution.py:139
  253.7 2.3 multiply_reduce_fusion.2
  262.9 2.3 multiply_reduce_fusion.2
  272.1 2.3 multiply_reduce_fusion.2
  281.3 2.3 multiply_reduce_fusion.2
  290.5 2.3 multiply_reduce_fusion.2
  316.3 2.3 reshape.284
  318.6 3.7 %all-to-all-start.1 = ((bf16[16,64,512]{2,1,0:T(8,128)(2,1)}), bf16[16,64,512]{2,1,0:T(8,128)(2,1)S(1)}, u32[]{:S(2)}, u32[]{:S(2)}) async-start(bf16[16,64,512]{2,1,0:T(8,128)(2,1)} %reshape.284), calls=%async_computation.2 | async-start | bytes 2097152 | tf_op jit(solution)/shard_map/all_to_all | solution.py:146
  322.2 18.2 %all-to-all-done.1 = bf16[16,64,512]{2,1,0:T(8,128)(2,1)S(1)} async-done(((bf16[16,64,512]{2,1,0:T(8,128)(2,1)}), bf16[16,64,512]{2,1,0:T(8,128)(2,1)S(1)}, u32[]{:S(2)}, u32[]{:S(2)}) %all-to-all-start.1) | async-done | bytes 1048608 | tf_op jit(solution)/shard_map/all_to_all | solution.py:146
  340.5 2.6 gather_fusion
  (197 shorter events, 79.4 us)
Async XLA Ops:
  6.5 192.1 %copy-start = (bf16[64,128,1,128]{3,1,2,0:T(8,128)(2,1)S(1)}, bf16[64,128,1,128]{3,1,2,0:T(8,128)(2,1)}, u32[]{:S(2)}) copy-start(bf16[64,128,1,128]{3,1,2,0:T(8,128)(2,1)} %param.19) | copy-start | bytes 6291460
  6.5 4.2 %copy-start.5 = (bf16[1024]{0:T(1024)(128)(2,1)S(1)}, bf16[1024]{0:T(1024)(128)(2,1)}, u32[]{:S(2)}) copy-start(bf16[1024]{0:T(1024)(128)(2,1)} %param.14) | copy-start | bytes 6148
  6.5 4.3 %copy-start.2 = (bf16[512,1024]{1,0:T(8,128)(2,1)S(1)}, bf16[512,1024]{1,0:T(8,128)(2,1)}, u32[]{:S(2)}) copy-start(bf16[512,1024]{1,0:T(8,128)(2,1)} %param.13) | copy-start | bytes 3145732
  6.5 96.0 %all-gather.3.cloned.1.call-start = ((), (), s32[]{:S(2)}) async-start(), calls=%async_computation.3 | async-start | bytes 13369344 | tf_op jit(solution)/shard_map/all_gather | solution.py:76
  10.7 176.0 %reduce-scatter.2.cloned.1.call-start = ((), (), s32[]{:S(2)}) async-start(), calls=%async_computation.4 | async-start | bytes 14155776 | tf_op jit(solution)/shard_map/reduce_scatter | solution.py:79
  191.4 7.2 %copy-start.6 = (s32[1,32]{1,0:T(1,128)S(1)}, s32[1,32]{1,0:T(1,128)}, u32[]{:S(2)}) copy-start(s32[1,32]{1,0:T(1,128)} %param.21) | copy-start | bytes 388
  191.4 35.2 %all-to-all-start = ((bf16[16,64,768]{2,1,0:T(8,128)(2,1)}), bf16[16,64,768]{2,1,0:T(8,128)(2,1)}, u32[]{:S(2)}, u32[]{:S(2)}) async-start(bf16[16,64,768]{2,1,0:T(8,128)(2,1)} %bitcast.112), calls=%async_computation.1 | async-start | bytes 3145728 | tf_op jit(solution)/shard_map/all_to_all | solution.py:94
  242.8 1.7 copy-start.1
  248.9 1.5 copy-start.3
  252.0 1.7 copy-start.1
  258.1 1.5 copy-start.3
  261.2 1.7 copy-start.1
  267.3 1.5 copy-start.3
  270.4 1.7 copy-start.1
  276.5 1.5 copy-start.3
  279.6 1.7 copy-start.1
  285.7 1.5 copy-start.3
  288.8 1.7 copy-start.1
  294.9 1.5 copy-start.3
  298.0 1.7 copy-start.1
  304.1 1.5 copy-start.3
  307.2 1.7 copy-start.1
  313.3 1.5 copy-start.3
  318.6 21.9 %all-to-all-start.1 = ((bf16[16,64,512]{2,1,0:T(8,128)(2,1)}), bf16[16,64,512]{2,1,0:T(8,128)(2,1)S(1)}, u32[]{:S(2)}, u32[]{:S(2)}) async-start(bf16[16,64,512]{2,1,0:T(8,128)(2,1)} %reshape.284), calls=%async_computation.2 | async-start | bytes 2097152 | tf_op jit(solution)/shard_map/all_to_all | solution.py:146
  (1 other events, 0.7 us)
Sparse Core Ops, SparseCore 0:
  10.9 91.6 all-gather.2
  117.1 69.6 reduce-scatter.1
where the time goes:
time: 351 us; the launch traced here: 350 us
  waiting for transfers between devices  159 us (45%)
  matrix products  62.2 us (18%)
  other arithmetic  38.3 us (11%)
  blocking collectives  35.5 us (10%)
  local copies, waits for them, and re-layouts  30.1 us (9%)
  between operations  13.6 us (4%)
  starting transfers between devices  10.9 us (3%)
    all_gather x1, waiting for transfers between devices, body(): gathered = lax.all_gather(weights_local, 'tok', axis=0, tiled=True)  78.9 us
    reduce_scatter x1, waiting for transfers between devices, body(): lax.psum_scatter(joined.reshape(group_count * row_count, joined.shape[2])...  43.5 us
    all_gather x1, blocking collectives, body(): lax.all_gather(group_of, 'tok', axis=0, tiled=True)  23 us
    all_to_all x1, waiting for transfers between devices, body(): lax.all_to_all(attended.reshape(n_tok, capacity, query_width), 'tok', spl...  18.2 us
    all_to_all x1, waiting for transfers between devices, body(): lax.all_to_all(outgoing.reshape(n_tok, capacity, width_all), 'tok', split...  18.2 us
    dot_general x8, matrix products, attend(): jnp.einsum('bhd,pd->bhp', queries, prefix_keys, preferred_element_type=jn...  18 us
    reduce_sum x16, other arithmetic, attend(): totals = jnp.sum(expo_before, axis=-1) + jnp.sum(expo_inside, axis=-1)  16.8 us
    dot_general x1, matrix products, body(): jnp.einsum('rd,dnc->nrc', normed, gathered, preferred_element_type=jnp.fl...  14.4 us
  transfers between devices with their start and end apart: 4, of which 4 were waited for; matrix products, arithmetic and copies ran while one was open for 4% of the time, Pallas kernels for 0%

commit v1 on v0

--- a/solution.py
+++ b/solution.py
@@ -6,6 +6,28 @@
 
 EPS = 1e-05
 THETA = 10000.0
+
+
+def laid_out(parts, dim):
+    dims = list(parts.shape[1:])
+    dims[dim] *= parts.shape[0]
+    return jnp.moveaxis(parts, 0, dim).reshape(dims)
+
+
+def gather_around(x, axis, dim):
+    size = lax.axis_size(axis)
+    pairs = [(i, (i + 1) % size) for i in range(size)]
+    back = [(b, a) for a, b in pairs]
+    lower, upper = ([], [])
+    for step in range(size - 1):
+        if step % 2 == 0:
+            lower.append(lax.ppermute(lower[-1] if lower else x, axis, pairs))
+        else:
+            upper.append(lax.ppermute(upper[-1] if upper else x, axis, back))
+    blocks = jnp.stack([*lower[::-1], x, *upper])
+    shift = lax.axis_index(axis) - len(lower)
+    blocks = blocks[(jnp.arange(size) - shift) % size]
+    return laid_out(blocks, dim)
 
 
 def rotate(values, positions):
@@ -94,7 +116,7 @@
     arrived = lax.all_to_all(
         outgoing.reshape(n_tok, capacity, width_all), "tok", split_axis=0, concat_axis=0, tiled=True
     )
-    all_groups = lax.all_gather(group_of, "tok", axis=0, tiled=True).reshape(n_tok, row_count)
+    all_groups = gather_around(group_of, "tok", 0).reshape(n_tok, row_count)
     block_counts = jnp.sum((all_groups == lax.axis_index("tok")).astype(jnp.int32), axis=1)
     slot_total = n_tok * capacity
     arrived = arrived.reshape(slot_total, width_all)

time: 351 us -> 352 us (level)
  starting transfers between devices: 10.9 us -> 52.2 us
  blocking collectives: 35.5 us -> 12.5 us
  waiting for transfers between devices: 159 us -> 141 us
    ppermute x0 -> x15, starting transfers between devices: none -> 38.4 us  [the longest x7 36.9 us: gather_around(): upper.append(lax.ppermute(upper[-1] if upper else x, axis, back))]
    ppermute x0 -> x15, waiting for transfers between devices: none -> 24.4 us  [the longest x7 22.7 us: gather_around(): upper.append(lax.ppermute(upper[-1] if upper else x, axis, back))]
    all_gather x1 -> x0, blocking collectives: 23 us -> none  [body(): lax.all_gather(group_of, 'tok', axis=0, tiled=True)]
    reduce_scatter x1, waiting for transfers between devices: 43.5 us -> 20.9 us  [body(): lax.psum_scatter(joined.reshape(group_count * row_count, joined.shape[2])...]
    all_to_all x1, waiting for transfers between devices: 18.2 us -> 0.01 us  [body(): lax.all_to_all(outgoing.reshape(n_tok, capacity, width_all), 'tok', split...]
  transfers between devices with their start and end apart: 4 -> 19, of which waited for: 4 -> 13; matrix products, arithmetic and copies ran while one was open for 4% -> 6% of each run, Pallas kernels for 0% -> 0%
where the time goes in v1:
time: 352 us; the launch traced here: 351 us
  waiting for transfers between devices  141 us (40%)
  matrix products  60.7 us (17%)
  starting transfers between devices  52.2 us (15%)
  other arithmetic  39.5 us (11%)
  local copies, waits for them, and re-layouts  31.4 us (9%)
  between operations  13.6 us (4%)
  blocking collectives  12.5 us (4%)
    all_gather x1, waiting for transfers between devices, body(): gathered = lax.all_gather(weights_local, 'tok', axis=0, tiled=True)  77.7 us
    ppermute x7, starting transfers between devices, gather_around(): upper.append(lax.ppermute(upper[-1] if upper else x, axis, back))  36.9 us
    ppermute x7, waiting for transfers between devices, gather_around(): upper.append(lax.ppermute(upper[-1] if upper else x, axis, back))  22.7 us
    reduce_scatter x1, waiting for transfers between devices, body(): lax.psum_scatter(joined.reshape(group_count * row_count, joined.shape[2])...  20.9 us
    dot_general x8, matrix products, attend(): jnp.einsum('bhd,pd->bhp', queries, prefix_keys, preferred_element_type=jn...  18 us
    all_to_all x1, waiting for transfers between devices, body(): lax.all_to_all(attended.reshape(n_tok, capacity, query_width), 'tok', spl...  17.8 us
    reduce_sum x16, other arithmetic, attend(): totals = jnp.sum(expo_before, axis=-1) + jnp.sum(expo_inside, axis=-1)  16.8 us
    dot_general x1, matrix products, body(): jnp.einsum('rd,dnc->nrc', normed, gathered, preferred_element_type=jnp.fl...  12.8 us
  transfers between devices with their start and end apart: 19, of which 13 were waited for; matrix products, arithmetic and copies ran while one was open for 6% of the time, Pallas kernels for 0%

profile of v1, /device:TPU:32, one launch (start us, length us, event | category | flops | bytes accessed | tf_op | source)
XLA Modules:
  0.0 351.0 jit_solution(12852378271746348801)
XLA Ops:
  12.3 12.5 %psum.7 = f32[512]{0:T(512)S(1)} all-reduce(f32[512]{0:T(512)S(1)} %fusion.33), channel_id=1, replica_groups=mesh['tok'=16,'head'=8] {'head'}, use_global_device_ids=true, to_apply=%region_4.5 | all-reduce | flops 512 | bytes 4096 | tf_op jit(solution)/shard_map/psum | solution.py:82
  24.8 77.7 %all-gather.2.cloned.1.call-done = bf16[1024,8,768]{2,0,1:T(8,128)(2,1)} async-done(((bf16[64,8,768]{2,0,1:T(8,128)(2,1)}), bf16[1024,8,768]{2,0,1:T(8,128)(2,1)}) %all-gather.2.cloned.1.call-update) | async-done | bytes 12582928 | tf_op jit(solution)/shard_map/all_gather | solution.py:98
  102.6 12.8 %fusion.41 = f32[8,768,512]{1,2,0:T(8,128)} fusion(bf16[1024,8,768]{2,0,1:T(8,128)(2,1)} %all-gather.2.cloned.1.call-done, bf16[512,1024]{1,0:T(8,128)(2,1)} %param.13, f32[1024]{0:T(1024)S(1)} %convert_element_type.75, f32[512]{0:T(512)S(1)} %add_rsqrt_fusion), kind=kOutput, calls=%fused_computation.59 | convolution fusion | flops 6444548096 | bytes 26220544 | tf_op jit(solution)/shard_map/rd,dnc->nrc/dot_general | solution.py:100
  117.6 3.9 %collective-permute-start.8 = (s32[512]{0:T(512)S(1)}, s32[512]{0:T(512)S(1)}, u32[]{:S(2)}, u32[]{:S(2)}) collective-permute-start(s32[512]{0:T(512)S(1)} %bitcast.138), channel_id=1, source_target_pairs={{8,0},{16,8},{24,16},{32,24},{40,32},{48,40},{56,48},{64,56},{72,6... | collective-permute-start | bytes 6152 | tf_op jit(solution)/shard_map/ppermute | solution.py:26
  123.1 3.9 %gather_fusion.3 = bf16[32,128,128]{2,1,0:T(8,128)(2,1)} fusion(bf16[64,128,128]{2,1,0:T(8,128)(2,1)} %bitcast.136, s32[1024]{0:T(1024)S(1)} %pad_clamp_fusion.1), kind=kCustom, calls=%fused_computation.1.clone | custom fusion | bytes 2097280 | tf_op jit(solution)/shard_map/jit(_take)/gather | solution.py:144
  127.0 2.8 broadcast_select_fusion
  131.0 5.4 %collective-permute-start.9 = (s32[512]{0:T(512)S(1)}, s32[512]{0:T(512)S(1)}, u32[]{:S(2)}, u32[]{:S(2)}) collective-permute-start(s32[512]{0:T(512)S(1)} %collective-permute-done.8), channel_id=1, source_target_pairs={{8,0},{16,8},{24,16},{32,24},{40,32},{48,40},{56,48},{64,56},{72,6... | collective-permute-start | bytes 6152 | tf_op jit(solution)/shard_map/ppermute | solution.py:26
  137.7 5.6 %collective-permute-start.10 = (s32[512]{0:T(512)S(1)}, s32[512]{0:T(512)S(1)}, u32[]{:S(2)}, u32[]{:S(2)}) collective-permute-start(s32[512]{0:T(512)S(1)} %collective-permute-done.9), channel_id=1, source_target_pairs={{8,0},{16,8},{24,16},{32,24},{40,32},{48,40},{56,48},{64,56},{72,6... | collective-permute-start | bytes 6152 | tf_op jit(solution)/shard_map/ppermute | solution.py:26
  144.6 5.6 %collective-permute-start.11 = (s32[512]{0:T(512)S(1)}, s32[512]{0:T(512)S(1)}, u32[]{:S(2)}, u32[]{:S(2)}) collective-permute-start(s32[512]{0:T(512)S(1)} %collective-permute-done.10), channel_id=1, source_target_pairs={{8,0},{16,8},{24,16},{32,24},{40,32},{48,40},{56,48},{64,56},{72,6... | collective-permute-start | bytes 6152 | tf_op jit(solution)/shard_map/ppermute | solution.py:26
  151.5 5.6 %collective-permute-start.12 = (s32[512]{0:T(512)S(1)}, s32[512]{0:T(512)S(1)}, u32[]{:S(2)}, u32[]{:S(2)}) collective-permute-start(s32[512]{0:T(512)S(1)} %collective-permute-done.11), channel_id=1, source_target_pairs={{8,0},{16,8},{24,16},{32,24},{40,32},{48,40},{56,48},{64,56},{72,6... | collective-permute-start | bytes 6152 | tf_op jit(solution)/shard_map/ppermute | solution.py:26
  158.4 5.6 %collective-permute-start.13 = (s32[512]{0:T(512)S(1)}, s32[512]{0:T(512)S(1)}, u32[]{:S(2)}, u32[]{:S(2)}) collective-permute-start(s32[512]{0:T(512)S(1)} %collective-permute-done.12), channel_id=1, source_target_pairs={{8,0},{16,8},{24,16},{32,24},{40,32},{48,40},{56,48},{64,56},{72,6... | collective-permute-start | bytes 6152 | tf_op jit(solution)/shard_map/ppermute | solution.py:26
  164.3 20.9 %reduce-scatter.2.cloned.1.call-done = f32[512,768]{1,0:T(8,128)} async-done(((f32[4096,768]{1,0:T(8,128)}), f32[512,768]{1,0:T(8,128)}) %reduce-scatter.2.cloned.1.call-update) | async-done | bytes 1572880 | tf_op jit(solution)/shard_map/reduce_scatter | solution.py:101
  185.2 4.6 %scatter_custom_fusion = bf16[1024,768]{1,0:T(8,128)(2,1)} fusion(s32[512]{0:T(512)S(1)} %bitcast.142, f32[512,768]{1,0:T(8,128)} %reduce-scatter.2.cloned.1.call-done, bf16[]{:T(256)} %constant.44.clone.1), kind=kCustom, calls=%fused_computation.66 | custom fusion | flops 393216 | bytes 3145730 | tf_op jit(solution)/shard_map/scatter | solution.py:114
  189.9 7.2 %all-to-all-start = ((bf16[16,64,768]{2,1,0:T(8,128)(2,1)}), bf16[16,64,768]{2,1,0:T(8,128)(2,1)}, u32[]{:S(2)}, u32[]{:S(2)}) async-start(bf16[16,64,768]{2,1,0:T(8,128)(2,1)} %bitcast.130), calls=%async_computation.1 | async-start | bytes 3145728 | tf_op jit(solution)/shard_map/all_to_all | solution.py:116
  197.2 5.3 %collective-permute-start.14 = (s32[512]{0:T(512)S(1)}, s32[512]{0:T(512)S(1)}, u32[]{:S(2)}, u32[]{:S(2)}) collective-permute-start(s32[512]{0:T(512)S(1)} %collective-permute-done.13), channel_id=1, source_target_pairs={{8,0},{16,8},{24,16},{32,24},{40,32},{48,40},{56,48},{64,56},{72,6... | collective-permute-start | bytes 6152 | tf_op jit(solution)/shard_map/ppermute | solution.py:26
  202.6 19.2 %collective-permute-done.14 = s32[512]{0:T(512)S(1)} collective-permute-done((s32[512]{0:T(512)S(1)}, s32[512]{0:T(512)S(1)}, u32[]{:S(2)}, u32[]{:S(2)}) %collective-permute-start.14) | collective-permute-done | bytes 2080 | tf_op jit(solution)/shard_map/ppermute | solution.py:26
  229.3 3.1 fusion.57
  232.5 2.3 copy.21
  237.7 2.4 copy.19
  241.3 73.7 %while.11 = (s32[]{:T(128)}, bf16[8,128,4,128]{3,2,1,0:T(4,128)(2,1)}, bf16[8,128,4,128]{3,1,2,0:T(8,128)(2,1)}, bf16[4096,128]{1,0:T(8,128)(2,1)}, s32[1024]{0:...) while((s32[]{:T(128)}, ...), condition=%wide.region_15.17_spmd.clone, body=%wide.region_10.16_spmd.clone.sunk | while | flops 1365182464 | bytes 41082088 | solution.py:161
  315.0 2.3 reshape.328
  317.3 6.5 %all-to-all-start.1 = ((bf16[16,64,512]{2,1,0:T(8,128)(2,1)}), bf16[16,64,512]{2,1,0:T(8,128)(2,1)S(1)}, u32[]{:S(2)}, u32[]{:S(2)}) async-start(bf16[16,64,512]{2,1,0:T(8,128)(2,1)} %reshape.328), calls=%async_computation.2 | async-start | bytes 2097152 | tf_op jit(solution)/shard_map/all_to_all | solution.py:168
  323.8 17.8 %all-to-all-done.1 = bf16[16,64,512]{2,1,0:T(8,128)(2,1)S(1)} async-done(((bf16[16,64,512]{2,1,0:T(8,128)(2,1)}), bf16[16,64,512]{2,1,0:T(8,128)(2,1)S(1)}, u32[]{:S(2)}, u32[]{:S(2)}) %all-to-all-start.1) | async-done | bytes 1048608 | tf_op jit(solution)/shard_map/all_to_all | solution.py:168
  341.6 2.6 gather_fusion.1
  (226 shorter events, 101.4 us)
Async XLA Ops:
  6.5 114.9 %copy-start = (bf16[64,128,1,128]{3,1,2,0:T(8,128)(2,1)S(1)}, bf16[64,128,1,128]{3,1,2,0:T(8,128)(2,1)}, u32[]{:S(2)}) copy-start(bf16[64,128,1,128]{3,1,2,0:T(8,128)(2,1)} %param.19) | copy-start | bytes 6291460
  6.5 4.3 %copy-start.4 = (bf16[1024]{0:T(1024)(128)(2,1)S(1)}, bf16[1024]{0:T(1024)(128)(2,1)}, u32[]{:S(2)}) copy-start(bf16[1024]{0:T(1024)(128)(2,1)} %param.14) | copy-start | bytes 6148
  6.5 96.0 %all-gather.2.cloned.1.call-start = ((), (), s32[]{:S(2)}) async-start(), calls=%async_computation.3 | async-start | bytes 13369344 | tf_op jit(solution)/shard_map/all_gather | solution.py:98
  10.7 174.5 %reduce-scatter.2.cloned.1.call-start = ((), (), s32[]{:S(2)}) async-start(), calls=%async_computation.4 | async-start | bytes 14155776 | tf_op jit(solution)/shard_map/reduce_scatter | solution.py:101
  115.4 6.0 %copy-start.5 = (s32[1,32]{1,0:T(1,128)S(1)}, s32[1,32]{1,0:T(1,128)}, u32[]{:S(2)}) copy-start(s32[1,32]{1,0:T(1,128)} %param.21) | copy-start | bytes 388
  116.1 13.7 %collective-permute-start = (s32[512]{0:T(512)S(1)}, s32[512]{0:T(512)S(1)}, u32[]{:S(2)}, u32[]{:S(2)}) collective-permute-start(s32[512]{0:T(512)S(1)} %bitcast.137), channel_id=1, source_target_pairs={{0,8},{8,16},{16,24},{24,32},{32,40},{40,48},{48,56},{56,64},{64,7... | collective-permute-start | bytes 6152 | tf_op jit(solution)/shard_map/ppermute | solution.py:24
  117.6 13.4 %collective-permute-start.8 = (s32[512]{0:T(512)S(1)}, s32[512]{0:T(512)S(1)}, u32[]{:S(2)}, u32[]{:S(2)}) collective-permute-start(s32[512]{0:T(512)S(1)} %bitcast.138), channel_id=1, source_target_pairs={{8,0},{16,8},{24,16},{32,24},{40,32},{48,40},{56,48},{64,56},{72,6... | collective-permute-start | bytes 6152 | tf_op jit(solution)/shard_map/ppermute | solution.py:26
  129.8 6.9 %collective-permute-start.1 = (s32[512]{0:T(512)S(1)}, s32[512]{0:T(512)S(1)}, u32[]{:S(2)}, u32[]{:S(2)}) collective-permute-start(s32[512]{0:T(512)S(1)} %collective-permute-done), channel_id=1, source_target_pairs={{0,8},{8,16},{16,24},{24,32},{32,40},{40,48},{48,56},{56,64},{64,7... | collective-permute-start | bytes 6152 | tf_op jit(solution)/shard_map/ppermute | solution.py:24
  131.0 6.7 %collective-permute-start.9 = (s32[512]{0:T(512)S(1)}, s32[512]{0:T(512)S(1)}, u32[]{:S(2)}, u32[]{:S(2)}) collective-permute-start(s32[512]{0:T(512)S(1)} %collective-permute-done.8), channel_id=1, source_target_pairs={{8,0},{16,8},{24,16},{32,24},{40,32},{48,40},{56,48},{64,56},{72,6... | collective-permute-start | bytes 6152 | tf_op jit(solution)/shard_map/ppermute | solution.py:26
  136.7 6.9 %collective-permute-start.2 = (s32[512]{0:T(512)S(1)}, s32[512]{0:T(512)S(1)}, u32[]{:S(2)}, u32[]{:S(2)}) collective-permute-start(s32[512]{0:T(512)S(1)} %collective-permute-done.1), channel_id=1, source_target_pairs={{0,8},{8,16},{16,24},{24,32},{32,40},{40,48},{48,56},{56,64},{64,7... | collective-permute-start | bytes 6152 | tf_op jit(solution)/shard_map/ppermute | solution.py:24
  137.7 6.9 %collective-permute-start.10 = (s32[512]{0:T(512)S(1)}, s32[512]{0:T(512)S(1)}, u32[]{:S(2)}, u32[]{:S(2)}) collective-permute-start(s32[512]{0:T(512)S(1)} %collective-permute-done.9), channel_id=1, source_target_pairs={{8,0},{16,8},{24,16},{32,24},{40,32},{48,40},{56,48},{64,56},{72,6... | collective-permute-start | bytes 6152 | tf_op jit(solution)/shard_map/ppermute | solution.py:26
  143.6 6.9 %collective-permute-start.3 = (s32[512]{0:T(512)S(1)}, s32[512]{0:T(512)S(1)}, u32[]{:S(2)}, u32[]{:S(2)}) collective-permute-start(s32[512]{0:T(512)S(1)} %collective-permute-done.2), channel_id=1, source_target_pairs={{0,8},{8,16},{16,24},{24,32},{32,40},{40,48},{48,56},{56,64},{64,7... | collective-permute-start | bytes 6152 | tf_op jit(solution)/shard_map/ppermute | solution.py:24
  144.6 6.9 %collective-permute-start.11 = (s32[512]{0:T(512)S(1)}, s32[512]{0:T(512)S(1)}, u32[]{:S(2)}, u32[]{:S(2)}) collective-permute-start(s32[512]{0:T(512)S(1)} %collective-permute-done.10), channel_id=1, source_target_pairs={{8,0},{16,8},{24,16},{32,24},{40,32},{48,40},{56,48},{64,56},{72,6... | collective-permute-start | bytes 6152 | tf_op jit(solution)/shard_map/ppermute | solution.py:26
  150.5 6.9 %collective-permute-start.4 = (s32[512]{0:T(512)S(1)}, s32[512]{0:T(512)S(1)}, u32[]{:S(2)}, u32[]{:S(2)}) collective-permute-start(s32[512]{0:T(512)S(1)} %collective-permute-done.3), channel_id=1, source_target_pairs={{0,8},{8,16},{16,24},{24,32},{32,40},{40,48},{48,56},{56,64},{64,7... | collective-permute-start | bytes 6152 | tf_op jit(solution)/shard_map/ppermute | solution.py:24
  151.5 6.9 %collective-permute-start.12 = (s32[512]{0:T(512)S(1)}, s32[512]{0:T(512)S(1)}, u32[]{:S(2)}, u32[]{:S(2)}) collective-permute-start(s32[512]{0:T(512)S(1)} %collective-permute-done.11), channel_id=1, source_target_pairs={{8,0},{16,8},{24,16},{32,24},{40,32},{48,40},{56,48},{64,56},{72,6... | collective-permute-start | bytes 6152 | tf_op jit(solution)/shard_map/ppermute | solution.py:26
  157.4 6.9 %collective-permute-start.5 = (s32[512]{0:T(512)S(1)}, s32[512]{0:T(512)S(1)}, u32[]{:S(2)}, u32[]{:S(2)}) collective-permute-start(s32[512]{0:T(512)S(1)} %collective-permute-done.4), channel_id=1, source_target_pairs={{0,8},{8,16},{16,24},{24,32},{32,40},{40,48},{48,56},{56,64},{64,7... | collective-permute-start | bytes 6152 | tf_op jit(solution)/shard_map/ppermute | solution.py:24
  158.4 38.8 %collective-permute-start.13 = (s32[512]{0:T(512)S(1)}, s32[512]{0:T(512)S(1)}, u32[]{:S(2)}, u32[]{:S(2)}) collective-permute-start(s32[512]{0:T(512)S(1)} %collective-permute-done.12), channel_id=1, source_target_pairs={{8,0},{16,8},{24,16},{32,24},{40,32},{48,40},{56,48},{64,56},{72,6... | collective-permute-start | bytes 6152 | tf_op jit(solution)/shard_map/ppermute | solution.py:26
  164.3 38.1 %collective-permute-start.6 = (s32[512]{0:T(512)S(1)}, s32[512]{0:T(512)S(1)}, u32[]{:S(2)}, u32[]{:S(2)}) collective-permute-start(s32[512]{0:T(512)S(1)} %collective-permute-done.5), channel_id=1, source_target_pairs={{0,8},{8,16},{16,24},{24,32},{32,40},{40,48},{48,56},{56,64},{64,7... | collective-permute-start | bytes 6152 | tf_op jit(solution)/shard_map/ppermute | solution.py:24
  189.9 35.4 %all-to-all-start = ((bf16[16,64,768]{2,1,0:T(8,128)(2,1)}), bf16[16,64,768]{2,1,0:T(8,128)(2,1)}, u32[]{:S(2)}, u32[]{:S(2)}) async-start(bf16[16,64,768]{2,1,0:T(8,128)(2,1)} %bitcast.130), calls=%async_computation.1 | async-start | bytes 3145728 | tf_op jit(solution)/shard_map/all_to_all | solution.py:116
  197.2 24.6 %collective-permute-start.14 = (s32[512]{0:T(512)S(1)}, s32[512]{0:T(512)S(1)}, u32[]{:S(2)}, u32[]{:S(2)}) collective-permute-start(s32[512]{0:T(512)S(1)} %collective-permute-done.13), channel_id=1, source_target_pairs={{8,0},{16,8},{24,16},{32,24},{40,32},{48,40},{56,48},{64,56},{72,6... | collective-permute-start | bytes 6152 | tf_op jit(solution)/shard_map/ppermute | solution.py:26
  202.4 19.3 %collective-permute-start.7 = (s32[512]{0:T(512)S(1)}, s32[512]{0:T(512)S(1)}, u32[]{:S(2)}, u32[]{:S(2)}) collective-permute-start(s32[512]{0:T(512)S(1)} %collective-permute-done.6), channel_id=1, source_target_pairs={{0,8},{8,16},{16,24},{24,32},{32,40},{40,48},{48,56},{56,64},{64,7... | collective-permute-start | bytes 6152 | tf_op jit(solution)/shard_map/ppermute | solution.py:24
  250.7 1.7 copy-start.1
  259.9 1.7 copy-start.1
  317.3 24.3 %all-to-all-start.1 = ((bf16[16,64,512]{2,1,0:T(8,128)(2,1)}), bf16[16,64,512]{2,1,0:T(8,128)(2,1)S(1)}, u32[]{:S(2)}, u32[]{:S(2)}) async-start(bf16[16,64,512]{2,1,0:T(8,128)(2,1)} %reshape.328), calls=%async_computation.2 | async-start | bytes 2097152 | tf_op jit(solution)/shard_map/all_to_all | solution.py:168
  (15 other events, 23.1 us)
Sparse Core Ops, SparseCore 0:
  10.9 91.6 all-gather.1
  115.5 69.6 reduce-scatter.1
